TPU v7x, 256 devices: a whole 4x4x8 slice. The times are simulated.
256 devices in a mesh: req: 32 (over z, x_lo, core), tp: 8 (over x_hi, y).
Axes of the slice: x: 4 (x_hi: 2, x_lo: 2; x = x_hi * 2 + x_lo), y: 4, z: 8, core: 2. Of those that a mesh axis runs over, the one named last changes fastest.
Arguments:
- queries: bfloat16 [12288, 8192], P('req', 'tp'), may hold values from -40 to 40
- suffix_kv: bfloat16 [2, 12288, 1024], P(None, 'req', 'tp'), may hold values from -4 to 4
- prefix_kv: bfloat16 [2, 32, 256, 1024], P(None, 'req', 'tp'), may hold values from -4 to 4
- suffix_length: int32 [31], replicated, may hold values from 16 to 384, as said below
- request_group: int32 [31], replicated, may hold values from 0 to 3
- request_order: int32 [31], replicated, may hold values from 0 to 30, each once
- owner_map: int32 [32], replicated, may hold values from 0 to 31, each once
Outputs:
- attention: bfloat16 [12288, 8192], P('req', 'tp')
Inputs may be any that keep to these rules, and one draw needn't show every extreme that they name: `suffix_length`: every suffix has 16 to 384 tokens; in every draw one suffix has exactly 384 tokens and one exactly 16.
All inputs are finite; a program needn't handle non-finite values.
Results may differ from a plain program's by a relative error of at most 0.007.
Values may be sent and summed in bfloat16 or wider, within the bound.
No kernel may reach another device: no remote copies, remote signals or barrier semaphores. Data moves between devices by JAX's collectives and lax.ppermute only.
A program may use at most 128 MiB of HBM per device.

v0:
```python
import math
import jax
import jax.numpy as jnp
from jax import lax
from jax.sharding import PartitionSpec as P

QH = 64
KVH = 8
HD = 128
GROUPS = 4
masked_score = -1e30


def from_behind(block, axis, distance):
    devices = range(lax.axis_size(axis))
    route = [(i - distance, i) for i in devices if i - distance in devices]
    return lax.ppermute(block, axis, route)


def pack_index(slot_ids, starts, stops):
    inside = (starts[None, :] <= slot_ids[:, None]) & (slot_ids[:, None] < stops[None, :])
    request_ids = jnp.arange(starts.shape[0], dtype=jnp.int32)
    found = jnp.sum(jnp.where(inside, request_ids[None, :], 0), axis=1)
    missing = jnp.where(jnp.any(inside, axis=1), 0, starts.shape[0]).astype(jnp.int32)
    return found + missing


def pick_rows(lookup, selector, extent):
    matches = selector[:, None] == jnp.arange(extent, dtype=jnp.int32)[None, :]
    return jnp.sum(jnp.where(matches, lookup[None, :], 0), axis=1)


def per_device(
    queries, suffix_kv, prefix_kv, suffix_length, request_group, request_order, owner_map
):
    tok_rows = queries.shape[0]
    head_cols = suffix_kv.shape[2]
    kv_heads = head_cols // HD
    per_kv = QH // KVH
    stored_count = owner_map.shape[0]
    per_group = stored_count // GROUPS
    requests = suffix_length.shape[0]
    score_scale = 1.0 / math.sqrt(HD)
    packed_length = pick_rows(suffix_length, request_order, requests)
    packed_group = pick_rows(request_group, request_order, requests)
    starts = (jnp.arange(requests, dtype=jnp.int32) + 1) * tok_rows - packed_length // 2
    stops = starts + packed_length
    device = lax.axis_index("req")
    slot_ids = device * tok_rows + jnp.arange(tok_rows, dtype=jnp.int32)
    own_pack = pack_index(slot_ids, starts, stops)
    is_live = own_pack < requests
    slot_group = pick_rows(packed_group, own_pack, requests)
    block_ids = jnp.arange(stored_count, dtype=jnp.int32)
    stored_group = jnp.sum(
        jnp.where(owner_map[None, :] == block_ids[:, None], (block_ids // per_group)[None, :], 0),
        axis=1,
    )
    query_heads = queries.reshape(tok_rows, kv_heads, per_kv, HD)

    def absorb(carried, key_rows, value_rows, allowed):
        running_max, running_sum, running_acc = carried
        scores = (
            jnp.einsum("tjqd,kjd->jtqk", query_heads, key_rows, preferred_element_type=jnp.float32)
            * score_scale
        )
        visible = allowed[None, :, None, :]
        scores = jnp.where(visible, scores, masked_score)
        new_max = jnp.maximum(running_max, jnp.max(scores, axis=-1))
        weights = jnp.where(visible, jnp.exp(scores - new_max[..., None]), 0.0)
        shrink = jnp.exp(running_max - new_max)
        new_sum = running_sum * shrink + jnp.sum(weights, axis=-1)
        product = jnp.einsum(
            "jtqk,kjd->jtqd",
            weights.astype(jnp.bfloat16),
            value_rows,
            preferred_element_type=jnp.float32,
        )
        return (new_max, new_sum, running_acc * shrink[..., None] + product)

    earlier = from_behind(suffix_kv, "req", 1)
    nearby = jnp.concatenate([earlier, suffix_kv], axis=1)
    near_slots = device * tok_rows - tok_rows + jnp.arange(2 * tok_rows, dtype=jnp.int32)
    near_pack = pack_index(near_slots, starts, stops)
    near_allowed = (
        (near_pack[None, :] == own_pack[:, None])
        & (near_slots[None, :] <= slot_ids[:, None])
        & (near_slots[None, :] >= 0)
        & is_live[:, None]
    )
    initial = (
        jnp.full((kv_heads, tok_rows, per_kv), masked_score, jnp.float32),
        jnp.zeros((kv_heads, tok_rows, per_kv), jnp.float32),
        jnp.zeros((kv_heads, tok_rows, per_kv, HD), jnp.float32),
    )
    carried = absorb(
        initial,
        nearby[0].reshape(2 * tok_rows, kv_heads, HD),
        nearby[1].reshape(2 * tok_rows, kv_heads, HD),
        near_allowed,
    )
    stored = lax.all_gather(prefix_kv, "req", axis=1, tiled=True)
    relaid = lax.all_to_all(stored, "tp", split_axis=3, concat_axis=2, tiled=True)
    status = carried
    extent = relaid.shape[1]
    block_rows = relaid.shape[2]
    stride = math.gcd(extent, max(1, 512 // block_rows))
    passes = extent // stride
    key_rows = relaid[0].reshape(passes, stride * block_rows, kv_heads, HD)
    value_rows = relaid[1].reshape(passes, stride * block_rows, kv_heads, HD)
    key_groups = jnp.repeat(stored_group, block_rows).reshape(passes, stride * block_rows)

    def visit_block(inner, inputs):
        keys_here, values_here, groups_here = inputs
        allowed = (groups_here[None, :] == slot_group[:, None]) & is_live[:, None]
        inner = absorb(inner, keys_here, values_here, allowed)
        return (inner, None)

    status, unused = lax.scan(visit_block, status, (key_rows, value_rows, key_groups))
    carried = status
    running_max, running_sum, running_acc = carried
    divisor = jnp.where(is_live[None, :, None], running_sum, 1.0)
    result = jnp.where(is_live[None, :, None, None], running_acc / divisor[..., None], 0.0)
    return (
        jnp.transpose(result, (1, 0, 2, 3))
        .reshape(tok_rows, kv_heads * per_kv * HD)
        .astype(jnp.bfloat16)
    )


def solution(mesh):
    in_specs = (
        P("req", "tp"),
        P(None, "req", "tp"),
        P(None, "req", "tp", None),
        P(),
        P(),
        P(),
        P(),
    )
    out_specs = P("req", "tp")
    return jax.shard_map(
        per_device, mesh=mesh, in_specs=in_specs, out_specs=out_specs, check_vma=False
    )
```

profile of v0, /device:TPU:1, one launch (start us, length us, event | category | flops | bytes accessed | tf_op | source)
XLA Modules:
  0.0 346.6 jit_solution(16441505130025673132)
XLA Ops:
  7.3 4.5 %collective-permute-start = (bf16[2,384,128]{2,1,0:T(8,128)(2,1)}, bf16[2,384,128]{2,1,0:T(8,128)(2,1)S(1)}, u32[]{:S(2)}, u32[]{:S(2)}) collective-permute-start(bf16[2,384,128]{2,1,0:T(8,128)(2,1)} %param.10), channel_id=1, source_target_pairs={{0,8},{8,16},{16,24},{24,32},{32,40},{40,48},{48,56},{56,64},{64,7... | collective-permute-start | bytes 589832 | tf_op jit(solution)/shard_map/ppermute | solution.py:17
  11.8 1.5 copy.45
  15.8 64.1 %all-gather.2.cloned.1.call-done = bf16[2,32,32,1024]{3,2,0,1:T(8,128)(2,1)} async-done(((bf16[2,1,32,1024]{3,2,0,1:T(8,128)(2,1)}), bf16[2,32,32,1024]{3,2,0,1:T(8,128)(2,1)}) %all-gather.2.cloned.1.call-update) | async-done | bytes 4194320 | tf_op jit(solution)/shard_map/all_gather | solution.py:101
  79.9 23.2 %copy.43 = bf16[2,32,32,1024]{2,1,0,3:T(8,128)(2,1)} copy(bf16[2,32,32,1024]{3,2,0,1:T(8,128)(2,1)} %all-gather.2.cloned.1.call-done) | data formatting | bytes 8388608 | tf_op jit(solution)/shard_map/all_gather | solution.py:101
  103.1 18.7 %reshape.344 = bf16[8,2,131072]{2,1,0:T(2,128)(2,1)} reshape(bf16[1024,2,32,32]{3,2,1,0:T(8,128)(2,1)} %bitcast.120) | data formatting | bytes 8388608
  121.8 6.3 %all-to-all-start = ((bf16[8,2,131072]{2,1,0:T(2,128)(2,1)}), bf16[8,2,131072]{2,1,0:T(2,128)(2,1)}, u32[]{:S(2)}, u32[]{:S(2)}) async-start(bf16[8,2,131072]{2,1,0:T(2,128)(2,1)} %reshape.344), calls=%async_computation | async-start | bytes 8388608 | tf_op jit(solution)/shard_map/all_to_all | solution.py:102
  129.1 1.6 fusion.20
  130.8 2.2 fusion.22
  133.1 4.0 %add_bitcast_fusion = f32[1,384,8,128]{3,1,2,0:T(8,128)} fusion(f32[768,384,8]{1,0,2:T(8,128)S(1)} %get-tuple-element.136, f32[384,8]{0,1:T(8,128)S(1)} %get-tuple-element.134, pred[384,768]{0,1:T(8,128)(4,1)S(1)} %and_and_fusion, f32[384,8]{0,1:T(8,128)S(1)} %get-tuple-element.132, bf16[2,768,128]{2,1,0:T(8,128)(2,1)S(1)} %constant_dynamic-update-slice_fusion), kind=kOutput, calls=%fused_computation.33 | convolution fusion | flops 616169472 | bytes 11526144 | tf_op jit(solution)/shard_map/jtqk,kjd->jtqd/dot_general | solution.py:72
  137.1 39.8 %all-to-all-done = bf16[8,2,131072]{2,1,0:T(2,128)(2,1)} async-done(((bf16[8,2,131072]{2,1,0:T(2,128)(2,1)}), bf16[8,2,131072]{2,1,0:T(2,128)(2,1)}, u32[]{:S(2)}, u32[]{:S(2)}) %all-to-all-start) | async-done | bytes 4194336 | tf_op jit(solution)/shard_map/all_to_all | solution.py:102
  176.8 12.4 %reshape.345 = bf16[1024,2,32,32]{3,2,1,0:T(8,128)(2,1)} reshape(bf16[8,2,131072]{2,1,0:T(2,128)(2,1)} %all-to-all-done) | data formatting | bytes 8388608
  189.3 12.6 %fusion.40 = (bf16[1,32,8,32,128]{3,1,0,4,2:T(8,128)(2,1)}, bf16[1,32,8,32,128]{3,1,0,4,2:T(8,128)(2,1)}) fusion(bf16[2,32,8,32,128]{3,1,0,4,2:T(8,128)(2,1)} %bitcast.121), kind=kLoop, calls=%fused_computation.80 | loop fusion | bytes 8388608 | tf_op jit(solution)/shard_map/slice | solution.py:109
  201.8 8.5 %copy.44 = bf16[1,32,8,32,128]{4,3,2,1,0:T(8,128)(2,1)S(1)} copy(bf16[1,32,8,32,128]{3,1,0,4,2:T(8,128)(2,1)} %get-tuple-element.131) | data formatting | bytes 4194304 | tf_op jit(solution)/shard_map/slice | solution.py:108
  210.3 9.3 %copy.46 = bf16[1,32,8,32,128]{4,3,2,1,0:T(8,128)(2,1)} copy(bf16[1,32,8,32,128]{3,1,0,4,2:T(8,128)(2,1)} %get-tuple-element.130) | data formatting | bytes 4194304 | tf_op jit(solution)/shard_map/slice | solution.py:109
  219.7 116.5 %while.14 = (s32[]{:T(128)}, f32[1,384,8]{1,2,0:T(8,128)S(1)}, f32[1,384,8]{1,2,0:T(8,128)S(1)}, f32[1,384,8,128]{3,1,2,0:T(8,128)}, s32[16,512]{1,0:T(8,128)S(1...) while((s32[]{:T(128)}, f32[1,384,8]{1,2,0:T(8,128)S(1)}, ...), condition=%wide.region_13.14_spmd, body=%wide.region_10.13_spmd.sunk | while | flops 826942464 | bytes 24060404 | solution.py:118
  221.0 4.4 %bitcast_add_fusion.6 = f32[1,384,8,128]{3,1,2,0:T(8,128)} fusion(f32[1,384,8,128]{3,1,2,0:T(8,128)} %get-tuple-element.220, f32[512,384,8]{1,0,2:T(8,128)S(1)} %get-tuple-element.204, f32[384,8]{0,1:T(8,128)S(1)} %bitcast.122, pred[384,512]{0,1:T(8,128)(4,1)S(1)} %compare_and_fusion.4, f32[384,8]{0,1:T(8,128)S(1)} %get-tuple-element.205, ...), kind=kOutput, calls=%fused_computation.7.clone.1 | convolution fusion | flops 411303936 | bytes 9789952 | tf_op jit(solution)/shard_map/while/body/eval_jaxpr/jtqk,kjd->jtqd/dot_general | solution.py:72
  225.4 1.5 fusion.51
  228.3 4.4 %bitcast_add_fusion.6 = f32[1,384,8,128]{3,1,2,0:T(8,128)} fusion(f32[1,384,8,128]{3,1,2,0:T(8,128)} %get-tuple-element.220, f32[512,384,8]{1,0,2:T(8,128)S(1)} %get-tuple-element.204, f32[384,8]{0,1:T(8,128)S(1)} %bitcast.122, pred[384,512]{0,1:T(8,128)(4,1)S(1)} %compare_and_fusion.4, f32[384,8]{0,1:T(8,128)S(1)} %get-tuple-element.205, ...), kind=kOutput, calls=%fused_computation.7.clone.1 | convolution fusion | flops 411303936 | bytes 9789952 | tf_op jit(solution)/shard_map/while/body/eval_jaxpr/jtqk,kjd->jtqd/dot_general | solution.py:72
  232.7 1.5 fusion.51
  235.6 4.4 %bitcast_add_fusion.6 = f32[1,384,8,128]{3,1,2,0:T(8,128)} fusion(f32[1,384,8,128]{3,1,2,0:T(8,128)} %get-tuple-element.220, f32[512,384,8]{1,0,2:T(8,128)S(1)} %get-tuple-element.204, f32[384,8]{0,1:T(8,128)S(1)} %bitcast.122, pred[384,512]{0,1:T(8,128)(4,1)S(1)} %compare_and_fusion.4, f32[384,8]{0,1:T(8,128)S(1)} %get-tuple-element.205, ...), kind=kOutput, calls=%fused_computation.7.clone.1 | convolution fusion | flops 411303936 | bytes 9789952 | tf_op jit(solution)/shard_map/while/body/eval_jaxpr/jtqk,kjd->jtqd/dot_general | solution.py:72
  239.9 1.5 fusion.51
  242.9 4.4 %bitcast_add_fusion.6 = f32[1,384,8,128]{3,1,2,0:T(8,128)} fusion(f32[1,384,8,128]{3,1,2,0:T(8,128)} %get-tuple-element.220, f32[512,384,8]{1,0,2:T(8,128)S(1)} %get-tuple-element.204, f32[384,8]{0,1:T(8,128)S(1)} %bitcast.122, pred[384,512]{0,1:T(8,128)(4,1)S(1)} %compare_and_fusion.4, f32[384,8]{0,1:T(8,128)S(1)} %get-tuple-element.205, ...), kind=kOutput, calls=%fused_computation.7.clone.1 | convolution fusion | flops 411303936 | bytes 9789952 | tf_op jit(solution)/shard_map/while/body/eval_jaxpr/jtqk,kjd->jtqd/dot_general | solution.py:72
  247.2 1.5 fusion.51
  250.2 4.4 %bitcast_add_fusion.6 = f32[1,384,8,128]{3,1,2,0:T(8,128)} fusion(f32[1,384,8,128]{3,1,2,0:T(8,128)} %get-tuple-element.220, f32[512,384,8]{1,0,2:T(8,128)S(1)} %get-tuple-element.204, f32[384,8]{0,1:T(8,128)S(1)} %bitcast.122, pred[384,512]{0,1:T(8,128)(4,1)S(1)} %compare_and_fusion.4, f32[384,8]{0,1:T(8,128)S(1)} %get-tuple-element.205, ...), kind=kOutput, calls=%fused_computation.7.clone.1 | convolution fusion | flops 411303936 | bytes 9789952 | tf_op jit(solution)/shard_map/while/body/eval_jaxpr/jtqk,kjd->jtqd/dot_general | solution.py:72
  254.5 1.5 fusion.51
  257.4 4.4 %bitcast_add_fusion.6 = f32[1,384,8,128]{3,1,2,0:T(8,128)} fusion(f32[1,384,8,128]{3,1,2,0:T(8,128)} %get-tuple-element.220, f32[512,384,8]{1,0,2:T(8,128)S(1)} %get-tuple-element.204, f32[384,8]{0,1:T(8,128)S(1)} %bitcast.122, pred[384,512]{0,1:T(8,128)(4,1)S(1)} %compare_and_fusion.4, f32[384,8]{0,1:T(8,128)S(1)} %get-tuple-element.205, ...), kind=kOutput, calls=%fused_computation.7.clone.1 | convolution fusion | flops 411303936 | bytes 9789952 | tf_op jit(solution)/shard_map/while/body/eval_jaxpr/jtqk,kjd->jtqd/dot_general | solution.py:72
  261.8 1.5 fusion.51
  264.7 4.4 %bitcast_add_fusion.6 = f32[1,384,8,128]{3,1,2,0:T(8,128)} fusion(f32[1,384,8,128]{3,1,2,0:T(8,128)} %get-tuple-element.220, f32[512,384,8]{1,0,2:T(8,128)S(1)} %get-tuple-element.204, f32[384,8]{0,1:T(8,128)S(1)} %bitcast.122, pred[384,512]{0,1:T(8,128)(4,1)S(1)} %compare_and_fusion.4, f32[384,8]{0,1:T(8,128)S(1)} %get-tuple-element.205, ...), kind=kOutput, calls=%fused_computation.7.clone.1 | convolution fusion | flops 411303936 | bytes 9789952 | tf_op jit(solution)/shard_map/while/body/eval_jaxpr/jtqk,kjd->jtqd/dot_general | solution.py:72
  269.1 1.5 fusion.51
  272.0 4.4 %bitcast_add_fusion.6 = f32[1,384,8,128]{3,1,2,0:T(8,128)} fusion(f32[1,384,8,128]{3,1,2,0:T(8,128)} %get-tuple-element.220, f32[512,384,8]{1,0,2:T(8,128)S(1)} %get-tuple-element.204, f32[384,8]{0,1:T(8,128)S(1)} %bitcast.122, pred[384,512]{0,1:T(8,128)(4,1)S(1)} %compare_and_fusion.4, f32[384,8]{0,1:T(8,128)S(1)} %get-tuple-element.205, ...), kind=kOutput, calls=%fused_computation.7.clone.1 | convolution fusion | flops 411303936 | bytes 9789952 | tf_op jit(solution)/shard_map/while/body/eval_jaxpr/jtqk,kjd->jtqd/dot_general | solution.py:72
  276.4 1.5 fusion.51
  279.3 4.4 %bitcast_add_fusion.6 = f32[1,384,8,128]{3,1,2,0:T(8,128)} fusion(f32[1,384,8,128]{3,1,2,0:T(8,128)} %get-tuple-element.220, f32[512,384,8]{1,0,2:T(8,128)S(1)} %get-tuple-element.204, f32[384,8]{0,1:T(8,128)S(1)} %bitcast.122, pred[384,512]{0,1:T(8,128)(4,1)S(1)} %compare_and_fusion.4, f32[384,8]{0,1:T(8,128)S(1)} %get-tuple-element.205, ...), kind=kOutput, calls=%fused_computation.7.clone.1 | convolution fusion | flops 411303936 | bytes 9789952 | tf_op jit(solution)/shard_map/while/body/eval_jaxpr/jtqk,kjd->jtqd/dot_general | solution.py:72
  283.7 1.5 fusion.51
  286.6 4.4 %bitcast_add_fusion.6 = f32[1,384,8,128]{3,1,2,0:T(8,128)} fusion(f32[1,384,8,128]{3,1,2,0:T(8,128)} %get-tuple-element.220, f32[512,384,8]{1,0,2:T(8,128)S(1)} %get-tuple-element.204, f32[384,8]{0,1:T(8,128)S(1)} %bitcast.122, pred[384,512]{0,1:T(8,128)(4,1)S(1)} %compare_and_fusion.4, f32[384,8]{0,1:T(8,128)S(1)} %get-tuple-element.205, ...), kind=kOutput, calls=%fused_computation.7.clone.1 | convolution fusion | flops 411303936 | bytes 9789952 | tf_op jit(solution)/shard_map/while/body/eval_jaxpr/jtqk,kjd->jtqd/dot_general | solution.py:72
  290.9 1.5 fusion.51
  293.9 4.4 %bitcast_add_fusion.6 = f32[1,384,8,128]{3,1,2,0:T(8,128)} fusion(f32[1,384,8,128]{3,1,2,0:T(8,128)} %get-tuple-element.220, f32[512,384,8]{1,0,2:T(8,128)S(1)} %get-tuple-element.204, f32[384,8]{0,1:T(8,128)S(1)} %bitcast.122, pred[384,512]{0,1:T(8,128)(4,1)S(1)} %compare_and_fusion.4, f32[384,8]{0,1:T(8,128)S(1)} %get-tuple-element.205, ...), kind=kOutput, calls=%fused_computation.7.clone.1 | convolution fusion | flops 411303936 | bytes 9789952 | tf_op jit(solution)/shard_map/while/body/eval_jaxpr/jtqk,kjd->jtqd/dot_general | solution.py:72
  298.2 1.5 fusion.51
  301.1 4.4 %bitcast_add_fusion.6 = f32[1,384,8,128]{3,1,2,0:T(8,128)} fusion(f32[1,384,8,128]{3,1,2,0:T(8,128)} %get-tuple-element.220, f32[512,384,8]{1,0,2:T(8,128)S(1)} %get-tuple-element.204, f32[384,8]{0,1:T(8,128)S(1)} %bitcast.122, pred[384,512]{0,1:T(8,128)(4,1)S(1)} %compare_and_fusion.4, f32[384,8]{0,1:T(8,128)S(1)} %get-tuple-element.205, ...), kind=kOutput, calls=%fused_computation.7.clone.1 | convolution fusion | flops 411303936 | bytes 9789952 | tf_op jit(solution)/shard_map/while/body/eval_jaxpr/jtqk,kjd->jtqd/dot_general | solution.py:72
  305.5 1.5 fusion.51
  308.4 4.4 %bitcast_add_fusion.6 = f32[1,384,8,128]{3,1,2,0:T(8,128)} fusion(f32[1,384,8,128]{3,1,2,0:T(8,128)} %get-tuple-element.220, f32[512,384,8]{1,0,2:T(8,128)S(1)} %get-tuple-element.204, f32[384,8]{0,1:T(8,128)S(1)} %bitcast.122, pred[384,512]{0,1:T(8,128)(4,1)S(1)} %compare_and_fusion.4, f32[384,8]{0,1:T(8,128)S(1)} %get-tuple-element.205, ...), kind=kOutput, calls=%fused_computation.7.clone.1 | convolution fusion | flops 411303936 | bytes 9789952 | tf_op jit(solution)/shard_map/while/body/eval_jaxpr/jtqk,kjd->jtqd/dot_general | solution.py:72
  312.8 1.5 fusion.51
  315.7 4.4 %bitcast_add_fusion.6 = f32[1,384,8,128]{3,1,2,0:T(8,128)} fusion(f32[1,384,8,128]{3,1,2,0:T(8,128)} %get-tuple-element.220, f32[512,384,8]{1,0,2:T(8,128)S(1)} %get-tuple-element.204, f32[384,8]{0,1:T(8,128)S(1)} %bitcast.122, pred[384,512]{0,1:T(8,128)(4,1)S(1)} %compare_and_fusion.4, f32[384,8]{0,1:T(8,128)S(1)} %get-tuple-element.205, ...), kind=kOutput, calls=%fused_computation.7.clone.1 | convolution fusion | flops 411303936 | bytes 9789952 | tf_op jit(solution)/shard_map/while/body/eval_jaxpr/jtqk,kjd->jtqd/dot_general | solution.py:72
  320.1 1.5 fusion.51
  323.0 4.4 %bitcast_add_fusion.6 = f32[1,384,8,128]{3,1,2,0:T(8,128)} fusion(f32[1,384,8,128]{3,1,2,0:T(8,128)} %get-tuple-element.220, f32[512,384,8]{1,0,2:T(8,128)S(1)} %get-tuple-element.204, f32[384,8]{0,1:T(8,128)S(1)} %bitcast.122, pred[384,512]{0,1:T(8,128)(4,1)S(1)} %compare_and_fusion.4, f32[384,8]{0,1:T(8,128)S(1)} %get-tuple-element.205, ...), kind=kOutput, calls=%fused_computation.7.clone.1 | convolution fusion | flops 411303936 | bytes 9789952 | tf_op jit(solution)/shard_map/while/body/eval_jaxpr/jtqk,kjd->jtqd/dot_general | solution.py:72
  327.4 1.5 fusion.51
  330.3 4.4 %bitcast_add_fusion.6 = f32[1,384,8,128]{3,1,2,0:T(8,128)} fusion(f32[1,384,8,128]{3,1,2,0:T(8,128)} %get-tuple-element.220, f32[512,384,8]{1,0,2:T(8,128)S(1)} %get-tuple-element.204, f32[384,8]{0,1:T(8,128)S(1)} %bitcast.122, pred[384,512]{0,1:T(8,128)(4,1)S(1)} %compare_and_fusion.4, f32[384,8]{0,1:T(8,128)S(1)} %get-tuple-element.205, ...), kind=kOutput, calls=%fused_computation.7.clone.1 | convolution fusion | flops 411303936 | bytes 9789952 | tf_op jit(solution)/shard_map/while/body/eval_jaxpr/jtqk,kjd->jtqd/dot_general | solution.py:72
  334.6 1.5 fusion.51
  336.2 1.9 select_convert_fusion
  (129 shorter events, 27.5 us)
Async XLA Ops:
  6.5 73.4 %all-gather.2.cloned.1.call-start = ((), (), s32[]{:S(2)}) async-start(), calls=%async_computation.1 | async-start | bytes 4325376 | tf_op jit(solution)/shard_map/all_gather | solution.py:101
  7.3 121.8 %collective-permute-start = (bf16[2,384,128]{2,1,0:T(8,128)(2,1)}, bf16[2,384,128]{2,1,0:T(8,128)(2,1)S(1)}, u32[]{:S(2)}, u32[]{:S(2)}) collective-permute-start(bf16[2,384,128]{2,1,0:T(8,128)(2,1)} %param.10), channel_id=1, source_target_pairs={{0,8},{8,16},{16,24},{24,32},{32,40},{40,48},{48,56},{56,64},{64,7... | collective-permute-start | bytes 589832 | tf_op jit(solution)/shard_map/ppermute | solution.py:17
  121.8 7.3 %copy-start.1 = (bf16[2,384,128]{2,1,0:T(8,128)(2,1)S(1)}, bf16[2,384,128]{2,1,0:T(8,128)(2,1)}, u32[]{:S(2)}) copy-start(bf16[2,384,128]{2,1,0:T(8,128)(2,1)} %param.10) | copy-start | bytes 589828
  121.8 7.3 %copy-start = (bf16[384,1024]{1,0:T(8,128)(2,1)S(1)}, bf16[384,1024]{1,0:T(8,128)(2,1)}, u32[]{:S(2)}) copy-start(bf16[384,1024]{1,0:T(8,128)(2,1)} %param.9) | copy-start | bytes 2359300
  121.8 55.0 %all-to-all-start = ((bf16[8,2,131072]{2,1,0:T(2,128)(2,1)}), bf16[8,2,131072]{2,1,0:T(2,128)(2,1)}, u32[]{:S(2)}, u32[]{:S(2)}) async-start(bf16[8,2,131072]{2,1,0:T(2,128)(2,1)} %reshape.344), calls=%async_computation | async-start | bytes 8388608 | tf_op jit(solution)/shard_map/all_to_all | solution.py:102
Sparse Core Ops, SparseCore 0:
  9.2 70.6 all-gather.1
where the time goes:
time: 348 us; the launch traced here: 347 us
  waiting for transfers between devices  105 us (30%)
  matrix products  93.4 us (27%)
  local copies, waits for them, and re-layouts  88.6 us (25%)
  other arithmetic  34.7 us (10%)
  between operations  13.6 us (4%)
  starting transfers between devices  10.8 us (3%)
    dot_general x17, matrix products, absorb(): jnp.einsum('jtqk,kjd->jtqd', weights.astype(jnp.bfloat16), value_rows, pr...  73.8 us
    all_gather x1, waiting for transfers between devices, per_device(): stored = lax.all_gather(prefix_kv, 'req', axis=1, tiled=True)  64.1 us
    all_to_all x1, waiting for transfers between devices, per_device(): lax.all_to_all(stored, 'tp', split_axis=3, concat_axis=2, tiled=True)  39.8 us
    unnamed x10, local copies, waits for them, and re-layouts  33.7 us
    reduce_sum x17, other arithmetic, absorb(): new_sum = running_sum * shrink + jnp.sum(weights, axis=-1)  26.4 us
    all_gather x1, local copies, waits for them, and re-layouts, per_device(): stored = lax.all_gather(prefix_kv, 'req', axis=1, tiled=True)  23.2 us
    slice x2, local copies, waits for them, and re-layouts, per_device(): value_rows = relaid[1].reshape(passes, stride * block_rows, kv_heads, HD)  21.9 us
    dot_general x17, matrix products, absorb(): jnp.einsum('tjqd,kjd->jtqk', query_heads, key_rows, preferred_element_typ...  19.6 us
  transfers between devices with their start and end apart: 3, of which 2 were waited for; matrix products, arithmetic and copies ran while one was open for 16% of the time, Pallas kernels for 0%

commit v1 on v0

--- a/solution.py
+++ b/solution.py
@@ -98,7 +98,9 @@
         nearby[1].reshape(2 * tok_rows, kv_heads, HD),
         near_allowed,
     )
-    stored = lax.all_gather(prefix_kv, "req", axis=1, tiled=True)
+    stored = jnp.concatenate(
+        lax.all_to_all(jnp.stack([prefix_kv] * lax.axis_size("req")), "req", 0, 0), axis=1
+    )
     relaid = lax.all_to_all(stored, "tp", split_axis=3, concat_axis=2, tiled=True)
     status = carried
     extent = relaid.shape[1]

time: 348 us -> 361 us (1.037)
  waiting for transfers between devices: 105 us -> 129 us
  between operations: 13.6 us -> 0.28 us
  starting transfers between devices: 10.8 us -> 21.1 us
  local copies, waits for them, and re-layouts: 88.6 us -> 80.6 us
    all_to_all x0 -> x1, waiting for transfers between devices: none -> 88.9 us  [per_device(): lax.all_to_all(jnp.stack([prefix_kv] * lax.axis_size('req')), 'req', 0, 0)]
    all_gather x1 -> x0, waiting for transfers between devices: 64.1 us -> none  [per_device(): stored = lax.all_gather(prefix_kv, 'req', axis=1, tiled=True)]
    reshape x0 -> x1, local copies, waits for them, and re-layouts: none -> 23.2 us  [per_device(): jnp.concatenate(lax.all_to_all(jnp.stack([prefix_kv] * lax.axis_size('req...]
    all_gather x1 -> x0, local copies, waits for them, and re-layouts: 23.2 us -> none  [per_device(): stored = lax.all_gather(prefix_kv, 'req', axis=1, tiled=True)]
    slice x2, local copies, waits for them, and re-layouts: 21.9 us -> 4.54 us  [per_device(): value_rows = relaid[1].reshape(passes, stride * block_rows, kv_heads, HD)]
    all_to_all x0 -> x1, local copies, waits for them, and re-layouts: none -> 15 us  [per_device(): lax.all_to_all(stored, 'tp', split_axis=3, concat_axis=2, tiled=True)]
    all_to_all x0 -> x1, starting transfers between devices: none -> 11.2 us  [per_device(): lax.all_to_all(jnp.stack([prefix_kv] * lax.axis_size('req')), 'req', 0, 0)]
    slice x1, local copies, waits for them, and re-layouts: 8.46 us -> 0.48 us  [per_device(): key_rows = relaid[0].reshape(passes, stride * block_rows, kv_heads, HD)]
  transfers between devices with their start and end apart: 3 -> 3, of which waited for: 2 -> 2; matrix products, arithmetic and copies ran while one was open for 16% -> 15% of each run, Pallas kernels for 0% -> 0%
where the time goes in v1:
time: 361 us; the launch traced here: 358 us
  waiting for transfers between devices  129 us (36%)
  matrix products  93.1 us (26%)
  local copies, waits for them, and re-layouts  80.6 us (22%)
  other arithmetic  33.4 us (9%)
  starting transfers between devices  21.1 us (6%)
    all_to_all x1, waiting for transfers between devices, per_device(): lax.all_to_all(jnp.stack([prefix_kv] * lax.axis_size('req')), 'req', 0, 0)  88.9 us
    dot_general x17, matrix products, absorb(): jnp.einsum('jtqk,kjd->jtqd', weights.astype(jnp.bfloat16), value_rows, pr...  73.5 us
    all_to_all x1, waiting for transfers between devices, per_device(): lax.all_to_all(stored, 'tp', split_axis=3, concat_axis=2, tiled=True)  39.8 us
    unnamed x18, local copies, waits for them, and re-layouts  32.6 us
    reduce_sum x17, other arithmetic, absorb(): new_sum = running_sum * shrink + jnp.sum(weights, axis=-1)  26.4 us
    reshape x1, local copies, waits for them, and re-layouts, per_device(): jnp.concatenate(lax.all_to_all(jnp.stack([prefix_kv] * lax.axis_size('req...  23.2 us
    dot_general x17, matrix products, absorb(): jnp.einsum('tjqd,kjd->jtqk', query_heads, key_rows, preferred_element_typ...  19.6 us
    all_to_all x1, local copies, waits for them, and re-layouts, per_device(): lax.all_to_all(stored, 'tp', split_axis=3, concat_axis=2, tiled=True)  15 us
  transfers between devices with their start and end apart: 3, of which 2 were waited for; matrix products, arithmetic and copies ran while one was open for 15% of the time, Pallas kernels for 0%

profile of v1, /device:TPU:1, one launch (start us, length us, event | category | flops | bytes accessed | tf_op | source)
XLA Modules:
  0.0 358.2 jit_solution(14062530535330527204)
XLA Ops:
  0.0 3.4 stack.2
  3.5 11.2 %all-to-all-start = ((bf16[32,2,1,32,1024]{4,3,1,2,0:T(8,128)(2,1)}), bf16[32,2,1,32,1024]{4,3,1,2,0:T(8,128)(2,1)}, u32[]{:S(2)}, u32[]{:S(2)}) async-start(bf16[32,2,1,32,1024]{4,3,1,2,0:T(8,128)(2,1)} %stack.2), calls=%async_computation | async-start | bytes 8388608 | tf_op jit(solution)/shard_map/all_to_all | solution.py:102
  14.7 3.5 collective-permute-start
  19.9 88.9 %all-to-all-done = bf16[32,2,1,32,1024]{4,3,1,2,0:T(8,128)(2,1)} async-done(((bf16[32,2,1,32,1024]{4,3,1,2,0:T(8,128)(2,1)}), bf16[32,2,1,32,1024]{4,3,1,2,0:T(8,128)(2,1)}, u32[]{:S(2)}, u32[]{:S(2)}) %all-to-all-start) | async-done | bytes 4194336 | tf_op jit(solution)/shard_map/all_to_all | solution.py:102
  108.8 23.2 %copy.43 = bf16[2,32,32,1024]{2,1,0,3:T(8,128)(2,1)} copy(bf16[2,32,32,1024]{3,2,0,1:T(8,128)(2,1)} %bitcast.22) | data formatting | bytes 8388608 | tf_op jit(solution)/shard_map/reshape | solution.py:101
  131.9 18.7 %reshape.355 = bf16[8,2,131072]{2,1,0:T(2,128)(2,1)} reshape(bf16[1024,2,32,32]{3,2,1,0:T(8,128)(2,1)} %bitcast.126) | data formatting | bytes 8388608
  150.7 6.4 %all-to-all-start.1 = ((bf16[8,2,131072]{2,1,0:T(2,128)(2,1)}), bf16[8,2,131072]{2,1,0:T(2,128)(2,1)}, u32[]{:S(2)}, u32[]{:S(2)}) async-start(bf16[8,2,131072]{2,1,0:T(2,128)(2,1)} %reshape.355), calls=%async_computation.1 | async-start | bytes 8388608 | tf_op jit(solution)/shard_map/all_to_all | solution.py:104
  158.1 1.6 fusion.20
  159.8 2.2 fusion.22
  162.0 4.0 %add_bitcast_fusion = f32[1,384,8,128]{3,1,2,0:T(8,128)} fusion(f32[768,384,8]{1,0,2:T(8,128)S(1)} %get-tuple-element.136, f32[384,8]{0,1:T(8,128)S(1)} %get-tuple-element.134, pred[384,768]{0,1:T(8,128)(4,1)S(1)} %and_and_fusion, f32[384,8]{0,1:T(8,128)S(1)} %get-tuple-element.132, bf16[2,768,128]{2,1,0:T(8,128)(2,1)S(1)} %constant_dynamic-update-slice_fusion), kind=kOutput, calls=%fused_computation.33 | convolution fusion | flops 616169472 | bytes 11526144 | tf_op jit(solution)/shard_map/jtqk,kjd->jtqd/dot_general | solution.py:72
  166.0 39.8 %all-to-all-done.1 = bf16[8,2,131072]{2,1,0:T(2,128)(2,1)} async-done(((bf16[8,2,131072]{2,1,0:T(2,128)(2,1)}), bf16[8,2,131072]{2,1,0:T(2,128)(2,1)}, u32[]{:S(2)}, u32[]{:S(2)}) %all-to-all-start.1) | async-done | bytes 4194336 | tf_op jit(solution)/shard_map/all_to_all | solution.py:104
  205.8 12.4 %reshape.356 = bf16[1024,2,32,32]{3,2,1,0:T(8,128)(2,1)} reshape(bf16[8,2,131072]{2,1,0:T(2,128)(2,1)} %all-to-all-done.1) | data formatting | bytes 8388608
  218.2 15.0 %copy.54 = bf16[2,32,32,8,128]{4,3,2,1,0:T(8,128)(2,1)} copy(bf16[2,32,32,8,128]{2,1,0,4,3:T(8,128)(2,1)} %bitcast.127) | data formatting | bytes 8388608 | tf_op jit(solution)/shard_map/all_to_all | solution.py:104
  233.3 2.7 fusion.40
  236.5 1.8 copy.47
  238.3 116.3 %while.14 = (s32[]{:T(128)}, f32[1,384,8]{1,2,0:T(8,128)S(1)}, f32[1,384,8]{1,2,0:T(8,128)S(1)}, f32[1,384,8,128]{3,1,2,0:T(8,128)}, s32[16,512]{1,0:T(8,128)S(1...) while((s32[]{:T(128)}, f32[1,384,8]{1,2,0:T(8,128)S(1)}, ...), condition=%wide.region_13.14_spmd, body=%wide.region_10.13_spmd.sunk | while | flops 826942464 | bytes 24060404 | solution.py:120
  239.7 4.3 %bitcast_add_fusion.6 = f32[1,384,8,128]{3,1,2,0:T(8,128)} fusion(f32[1,384,8,128]{3,1,2,0:T(8,128)} %get-tuple-element.220, f32[512,384,8]{1,0,2:T(8,128)S(1)} %get-tuple-element.204, f32[384,8]{0,1:T(8,128)S(1)} %bitcast.129, pred[384,512]{0,1:T(8,128)(4,1)S(1)} %compare_and_fusion.4, f32[384,8]{0,1:T(8,128)S(1)} %get-tuple-element.205, ...), kind=kOutput, calls=%fused_computation.7.clone.1 | convolution fusion | flops 411303936 | bytes 9789952 | tf_op jit(solution)/shard_map/while/body/eval_jaxpr/jtqk,kjd->jtqd/dot_general | solution.py:72
  244.0 1.5 fusion.51
  246.9 4.3 %bitcast_add_fusion.6 = f32[1,384,8,128]{3,1,2,0:T(8,128)} fusion(f32[1,384,8,128]{3,1,2,0:T(8,128)} %get-tuple-element.220, f32[512,384,8]{1,0,2:T(8,128)S(1)} %get-tuple-element.204, f32[384,8]{0,1:T(8,128)S(1)} %bitcast.129, pred[384,512]{0,1:T(8,128)(4,1)S(1)} %compare_and_fusion.4, f32[384,8]{0,1:T(8,128)S(1)} %get-tuple-element.205, ...), kind=kOutput, calls=%fused_computation.7.clone.1 | convolution fusion | flops 411303936 | bytes 9789952 | tf_op jit(solution)/shard_map/while/body/eval_jaxpr/jtqk,kjd->jtqd/dot_general | solution.py:72
  251.3 1.5 fusion.51
  254.2 4.3 %bitcast_add_fusion.6 = f32[1,384,8,128]{3,1,2,0:T(8,128)} fusion(f32[1,384,8,128]{3,1,2,0:T(8,128)} %get-tuple-element.220, f32[512,384,8]{1,0,2:T(8,128)S(1)} %get-tuple-element.204, f32[384,8]{0,1:T(8,128)S(1)} %bitcast.129, pred[384,512]{0,1:T(8,128)(4,1)S(1)} %compare_and_fusion.4, f32[384,8]{0,1:T(8,128)S(1)} %get-tuple-element.205, ...), kind=kOutput, calls=%fused_computation.7.clone.1 | convolution fusion | flops 411303936 | bytes 9789952 | tf_op jit(solution)/shard_map/while/body/eval_jaxpr/jtqk,kjd->jtqd/dot_general | solution.py:72
  258.6 1.5 fusion.51
  261.5 4.3 %bitcast_add_fusion.6 = f32[1,384,8,128]{3,1,2,0:T(8,128)} fusion(f32[1,384,8,128]{3,1,2,0:T(8,128)} %get-tuple-element.220, f32[512,384,8]{1,0,2:T(8,128)S(1)} %get-tuple-element.204, f32[384,8]{0,1:T(8,128)S(1)} %bitcast.129, pred[384,512]{0,1:T(8,128)(4,1)S(1)} %compare_and_fusion.4, f32[384,8]{0,1:T(8,128)S(1)} %get-tuple-element.205, ...), kind=kOutput, calls=%fused_computation.7.clone.1 | convolution fusion | flops 411303936 | bytes 9789952 | tf_op jit(solution)/shard_map/while/body/eval_jaxpr/jtqk,kjd->jtqd/dot_general | solution.py:72
  265.8 1.5 fusion.51
  268.7 4.3 %bitcast_add_fusion.6 = f32[1,384,8,128]{3,1,2,0:T(8,128)} fusion(f32[1,384,8,128]{3,1,2,0:T(8,128)} %get-tuple-element.220, f32[512,384,8]{1,0,2:T(8,128)S(1)} %get-tuple-element.204, f32[384,8]{0,1:T(8,128)S(1)} %bitcast.129, pred[384,512]{0,1:T(8,128)(4,1)S(1)} %compare_and_fusion.4, f32[384,8]{0,1:T(8,128)S(1)} %get-tuple-element.205, ...), kind=kOutput, calls=%fused_computation.7.clone.1 | convolution fusion | flops 411303936 | bytes 9789952 | tf_op jit(solution)/shard_map/while/body/eval_jaxpr/jtqk,kjd->jtqd/dot_general | solution.py:72
  273.1 1.5 fusion.51
  276.0 4.3 %bitcast_add_fusion.6 = f32[1,384,8,128]{3,1,2,0:T(8,128)} fusion(f32[1,384,8,128]{3,1,2,0:T(8,128)} %get-tuple-element.220, f32[512,384,8]{1,0,2:T(8,128)S(1)} %get-tuple-element.204, f32[384,8]{0,1:T(8,128)S(1)} %bitcast.129, pred[384,512]{0,1:T(8,128)(4,1)S(1)} %compare_and_fusion.4, f32[384,8]{0,1:T(8,128)S(1)} %get-tuple-element.205, ...), kind=kOutput, calls=%fused_computation.7.clone.1 | convolution fusion | flops 411303936 | bytes 9789952 | tf_op jit(solution)/shard_map/while/body/eval_jaxpr/jtqk,kjd->jtqd/dot_general | solution.py:72
  280.4 1.5 fusion.51
  283.3 4.3 %bitcast_add_fusion.6 = f32[1,384,8,128]{3,1,2,0:T(8,128)} fusion(f32[1,384,8,128]{3,1,2,0:T(8,128)} %get-tuple-element.220, f32[512,384,8]{1,0,2:T(8,128)S(1)} %get-tuple-element.204, f32[384,8]{0,1:T(8,128)S(1)} %bitcast.129, pred[384,512]{0,1:T(8,128)(4,1)S(1)} %compare_and_fusion.4, f32[384,8]{0,1:T(8,128)S(1)} %get-tuple-element.205, ...), kind=kOutput, calls=%fused_computation.7.clone.1 | convolution fusion | flops 411303936 | bytes 9789952 | tf_op jit(solution)/shard_map/while/body/eval_jaxpr/jtqk,kjd->jtqd/dot_general | solution.py:72
  287.6 1.5 fusion.51
  290.6 4.3 %bitcast_add_fusion.6 = f32[1,384,8,128]{3,1,2,0:T(8,128)} fusion(f32[1,384,8,128]{3,1,2,0:T(8,128)} %get-tuple-element.220, f32[512,384,8]{1,0,2:T(8,128)S(1)} %get-tuple-element.204, f32[384,8]{0,1:T(8,128)S(1)} %bitcast.129, pred[384,512]{0,1:T(8,128)(4,1)S(1)} %compare_and_fusion.4, f32[384,8]{0,1:T(8,128)S(1)} %get-tuple-element.205, ...), kind=kOutput, calls=%fused_computation.7.clone.1 | convolution fusion | flops 411303936 | bytes 9789952 | tf_op jit(solution)/shard_map/while/body/eval_jaxpr/jtqk,kjd->jtqd/dot_general | solution.py:72
  294.9 1.5 fusion.51
  297.8 4.3 %bitcast_add_fusion.6 = f32[1,384,8,128]{3,1,2,0:T(8,128)} fusion(f32[1,384,8,128]{3,1,2,0:T(8,128)} %get-tuple-element.220, f32[512,384,8]{1,0,2:T(8,128)S(1)} %get-tuple-element.204, f32[384,8]{0,1:T(8,128)S(1)} %bitcast.129, pred[384,512]{0,1:T(8,128)(4,1)S(1)} %compare_and_fusion.4, f32[384,8]{0,1:T(8,128)S(1)} %get-tuple-element.205, ...), kind=kOutput, calls=%fused_computation.7.clone.1 | convolution fusion | flops 411303936 | bytes 9789952 | tf_op jit(solution)/shard_map/while/body/eval_jaxpr/jtqk,kjd->jtqd/dot_general | solution.py:72
  302.2 1.5 fusion.51
  305.1 4.3 %bitcast_add_fusion.6 = f32[1,384,8,128]{3,1,2,0:T(8,128)} fusion(f32[1,384,8,128]{3,1,2,0:T(8,128)} %get-tuple-element.220, f32[512,384,8]{1,0,2:T(8,128)S(1)} %get-tuple-element.204, f32[384,8]{0,1:T(8,128)S(1)} %bitcast.129, pred[384,512]{0,1:T(8,128)(4,1)S(1)} %compare_and_fusion.4, f32[384,8]{0,1:T(8,128)S(1)} %get-tuple-element.205, ...), kind=kOutput, calls=%fused_computation.7.clone.1 | convolution fusion | flops 411303936 | bytes 9789952 | tf_op jit(solution)/shard_map/while/body/eval_jaxpr/jtqk,kjd->jtqd/dot_general | solution.py:72
  309.5 1.5 fusion.51
  312.4 4.3 %bitcast_add_fusion.6 = f32[1,384,8,128]{3,1,2,0:T(8,128)} fusion(f32[1,384,8,128]{3,1,2,0:T(8,128)} %get-tuple-element.220, f32[512,384,8]{1,0,2:T(8,128)S(1)} %get-tuple-element.204, f32[384,8]{0,1:T(8,128)S(1)} %bitcast.129, pred[384,512]{0,1:T(8,128)(4,1)S(1)} %compare_and_fusion.4, f32[384,8]{0,1:T(8,128)S(1)} %get-tuple-element.205, ...), kind=kOutput, calls=%fused_computation.7.clone.1 | convolution fusion | flops 411303936 | bytes 9789952 | tf_op jit(solution)/shard_map/while/body/eval_jaxpr/jtqk,kjd->jtqd/dot_general | solution.py:72
  316.7 1.5 fusion.51
  319.6 4.3 %bitcast_add_fusion.6 = f32[1,384,8,128]{3,1,2,0:T(8,128)} fusion(f32[1,384,8,128]{3,1,2,0:T(8,128)} %get-tuple-element.220, f32[512,384,8]{1,0,2:T(8,128)S(1)} %get-tuple-element.204, f32[384,8]{0,1:T(8,128)S(1)} %bitcast.129, pred[384,512]{0,1:T(8,128)(4,1)S(1)} %compare_and_fusion.4, f32[384,8]{0,1:T(8,128)S(1)} %get-tuple-element.205, ...), kind=kOutput, calls=%fused_computation.7.clone.1 | convolution fusion | flops 411303936 | bytes 9789952 | tf_op jit(solution)/shard_map/while/body/eval_jaxpr/jtqk,kjd->jtqd/dot_general | solution.py:72
  324.0 1.5 fusion.51
  326.9 4.3 %bitcast_add_fusion.6 = f32[1,384,8,128]{3,1,2,0:T(8,128)} fusion(f32[1,384,8,128]{3,1,2,0:T(8,128)} %get-tuple-element.220, f32[512,384,8]{1,0,2:T(8,128)S(1)} %get-tuple-element.204, f32[384,8]{0,1:T(8,128)S(1)} %bitcast.129, pred[384,512]{0,1:T(8,128)(4,1)S(1)} %compare_and_fusion.4, f32[384,8]{0,1:T(8,128)S(1)} %get-tuple-element.205, ...), kind=kOutput, calls=%fused_computation.7.clone.1 | convolution fusion | flops 411303936 | bytes 9789952 | tf_op jit(solution)/shard_map/while/body/eval_jaxpr/jtqk,kjd->jtqd/dot_general | solution.py:72
  331.3 1.5 fusion.51
  334.2 4.3 %bitcast_add_fusion.6 = f32[1,384,8,128]{3,1,2,0:T(8,128)} fusion(f32[1,384,8,128]{3,1,2,0:T(8,128)} %get-tuple-element.220, f32[512,384,8]{1,0,2:T(8,128)S(1)} %get-tuple-element.204, f32[384,8]{0,1:T(8,128)S(1)} %bitcast.129, pred[384,512]{0,1:T(8,128)(4,1)S(1)} %compare_and_fusion.4, f32[384,8]{0,1:T(8,128)S(1)} %get-tuple-element.205, ...), kind=kOutput, calls=%fused_computation.7.clone.1 | convolution fusion | flops 411303936 | bytes 9789952 | tf_op jit(solution)/shard_map/while/body/eval_jaxpr/jtqk,kjd->jtqd/dot_general | solution.py:72
  338.5 1.5 fusion.51
  341.5 4.3 %bitcast_add_fusion.6 = f32[1,384,8,128]{3,1,2,0:T(8,128)} fusion(f32[1,384,8,128]{3,1,2,0:T(8,128)} %get-tuple-element.220, f32[512,384,8]{1,0,2:T(8,128)S(1)} %get-tuple-element.204, f32[384,8]{0,1:T(8,128)S(1)} %bitcast.129, pred[384,512]{0,1:T(8,128)(4,1)S(1)} %compare_and_fusion.4, f32[384,8]{0,1:T(8,128)S(1)} %get-tuple-element.205, ...), kind=kOutput, calls=%fused_computation.7.clone.1 | convolution fusion | flops 411303936 | bytes 9789952 | tf_op jit(solution)/shard_map/while/body/eval_jaxpr/jtqk,kjd->jtqd/dot_general | solution.py:72
  348.7 4.3 %bitcast_add_fusion.6 = f32[1,384,8,128]{3,1,2,0:T(8,128)} fusion(f32[1,384,8,128]{3,1,2,0:T(8,128)} %get-tuple-element.220, f32[512,384,8]{1,0,2:T(8,128)S(1)} %get-tuple-element.204, f32[384,8]{0,1:T(8,128)S(1)} %bitcast.129, pred[384,512]{0,1:T(8,128)(4,1)S(1)} %compare_and_fusion.4, f32[384,8]{0,1:T(8,128)S(1)} %get-tuple-element.205, ...), kind=kOutput, calls=%fused_computation.7.clone.1 | convolution fusion | flops 411303936 | bytes 9789952 | tf_op jit(solution)/shard_map/while/body/eval_jaxpr/jtqk,kjd->jtqd/dot_general | solution.py:72
  353.1 1.5 fusion.51
  354.6 1.9 select_convert_fusion
  (138 shorter events, 27.8 us)
Async XLA Ops:
  0.0 14.7 %copy-start.1 = (bf16[2,384,128]{2,1,0:T(8,128)(2,1)S(1)}, bf16[2,384,128]{2,1,0:T(8,128)(2,1)}, u32[]{:S(2)}) copy-start(bf16[2,384,128]{2,1,0:T(8,128)(2,1)} %param.10) | copy-start | bytes 589828
  0.0 18.3 %copy-start = (bf16[384,1024]{1,0:T(8,128)(2,1)S(1)}, bf16[384,1024]{1,0:T(8,128)(2,1)}, u32[]{:S(2)}) copy-start(bf16[384,1024]{1,0:T(8,128)(2,1)} %param.9) | copy-start | bytes 2359300
  3.4 15.6 %copy-start.5 = (s32[32]{0:T(128)S(1)}, s32[32]{0:T(128)}, u32[]{:S(2)}) copy-start(s32[32]{0:T(128)} %param.15) | copy-start | bytes 388
  3.5 15.9 %copy-start.2 = (s32[31]{0:T(128)S(1)}, s32[31]{0:T(128)}, u32[]{:S(2)}) copy-start(s32[31]{0:T(128)} %param.13) | copy-start | bytes 376
  3.5 15.9 %copy-start.3 = (s32[31]{0:T(128)S(1)}, s32[31]{0:T(128)}, u32[]{:S(2)}) copy-start(s32[31]{0:T(128)} %param.14) | copy-start | bytes 376
  3.5 16.0 %copy-start.4 = (s32[31]{0:T(128)S(1)}, s32[31]{0:T(128)}, u32[]{:S(2)}) copy-start(s32[31]{0:T(128)} %param.12) | copy-start | bytes 376
  3.5 105.3 %all-to-all-start = ((bf16[32,2,1,32,1024]{4,3,1,2,0:T(8,128)(2,1)}), bf16[32,2,1,32,1024]{4,3,1,2,0:T(8,128)(2,1)}, u32[]{:S(2)}, u32[]{:S(2)}) async-start(bf16[32,2,1,32,1024]{4,3,1,2,0:T(8,128)(2,1)} %stack.2), calls=%async_computation | async-start | bytes 8388608 | tf_op jit(solution)/shard_map/all_to_all | solution.py:102
  14.7 143.3 %collective-permute-start = (bf16[2,384,128]{2,1,0:T(8,128)(2,1)S(1)}, bf16[2,384,128]{2,1,0:T(8,128)(2,1)S(1)}, u32[]{:S(2)}, u32[]{:S(2)}) collective-permute-start(bf16[2,384,128]{2,1,0:T(8,128)(2,1)S(1)} %copy-done.1), channel_id=1, source_target_pairs={{0,8},{8,16},{16,24},{24,32},{32,40},{40,48},{48,56},{56,64},{64,7... | collective-permute-start | bytes 589832 | tf_op jit(solution)/shard_map/ppermute | solution.py:17
  150.7 55.1 %all-to-all-start.1 = ((bf16[8,2,131072]{2,1,0:T(2,128)(2,1)}), bf16[8,2,131072]{2,1,0:T(2,128)(2,1)}, u32[]{:S(2)}, u32[]{:S(2)}) async-start(bf16[8,2,131072]{2,1,0:T(2,128)(2,1)} %reshape.355), calls=%async_computation.1 | async-start | bytes 8388608 | tf_op jit(solution)/shard_map/all_to_all | solution.py:104
